TPU v7x, 32 devices: a whole 2x2x4 slice. The times are simulated.
32 devices in a mesh: gx: 8 (over z, x), gy: 4 (over y, core).
Axes of the slice: x: 2, y: 2, z: 4, core: 2. Of those that a mesh axis runs over, the one named last changes fastest.
Arguments:
- inputs: bfloat16 [3, 256, 8192], P(None, 'gy', 'gx'), may hold values from -600 to 600
- norm_gain: bfloat16 [8192], P('gx'), may hold values from 0.099609375 to 1.8984375
- query_weight: bfloat16 [8192, 8192], P('gx', 'gy'), may hold values from -0.0625 to 0.0625
- key_weight: bfloat16 [8192, 1024], P('gx', 'gy'), may hold values from -0.0625 to 0.0625
- value_weight: bfloat16 [8192, 1024], P('gx', 'gy'), may hold values from -0.0625 to 0.0625
- output_weight: bfloat16 [8192, 8192], P('gy', 'gx'), may hold values from -0.0625 to 0.0625
- query_down: bfloat16 [256, 8192, 64], P('gy', 'gx'), may hold values from -0.0625 to 0.0625
- query_up: bfloat16 [256, 64, 8192], P('gx', None, 'gy'), may hold values from -0.75 to 0.75
- output_down: bfloat16 [256, 8192, 64], P('gx', 'gy'), may hold values from -0.0625 to 0.0625
- output_up: bfloat16 [256, 64, 8192], P('gy', None, 'gx'), may hold values from -0.75 to 0.75
- block_adapter: int32 [2], replicated, may hold values from 0 to 255
- cache_lengths: int32 [256], P(('gx', 'gy')), may hold values from 1 to 256, as said below
- cache_keys: bfloat16 [256, 256, 1024], P(('gx', 'gy')), may hold values from -160 to 160
- cache_values: bfloat16 [256, 256, 1024], P(('gx', 'gy')), may hold values from -6 to 6
Outputs:
- block_output: bfloat16 [3, 256, 8192], P(None, 'gy', 'gx')
Inputs may be any that keep to these rules, and one draw needn't show every extreme that they name: `cache_lengths`: some request has exactly 256 cached positions.
All inputs are finite; a program needn't handle non-finite values.
Results may differ from a plain program's by a relative error of at most 0.012.
The roundings to bfloat16 on the way count: a program that leaves them out, or rounds other values in their place, can miss the bound.
Values may be sent and summed in bfloat16 or wider, within the bound.
No kernel may reach another device: no remote copies, remote signals or barrier semaphores. Data moves between devices by JAX's collectives and lax.ppermute only.
A program may use at most 192 MiB of HBM per device.

v0:
```python
import jax
import jax.numpy as jnp
from jax import lax
from jax.sharding import PartitionSpec as P

D = 8192
QUERY_HEADS = 64
KEY_VALUE_HEADS = 8
HEAD_FEATURES = 128
BLOCK = 128
STEPS = 3
EPS = 1e-05
THETA = 500000.0


def rotary_embedding(values_in, token_positions):
    half_size = values_in.shape[-1] // 2
    exponent = jnp.arange(half_size, dtype=jnp.float32) * 2.0 / values_in.shape[-1]
    frequency = THETA ** (-exponent)
    angles = token_positions.astype(jnp.float32)[:, None] * frequency[None, :]
    cosine = jnp.cos(angles)[:, None, :]
    sine_part = jnp.sin(angles)[:, None, :]
    lower = values_in[..., :half_size]
    upper = values_in[..., half_size:]
    return jnp.concatenate(
        [lower * cosine - upper * sine_part, upper * cosine + lower * sine_part], axis=-1
    )


def pick_adapters(table, adapter_ids, first_id):
    table_count = table.shape[0]
    wanted = first_id + jnp.arange(table_count, dtype=jnp.int32)
    onehot = (adapter_ids[:, None] == wanted[None, :]).astype(table.dtype)
    flat_table = table.reshape(table_count, -1)
    picked = jnp.dot(onehot, flat_table, preferred_element_type=jnp.float32).astype(table.dtype)
    return picked.reshape((adapter_ids.shape[0],) + table.shape[1:])


def attend(
    query_rows, previous_keys, previous_values, incoming_keys, incoming_values, lengths, step_index
):
    count_of_rows = query_rows.shape[0]
    context_window = previous_keys.shape[1]
    grouped_heads = query_rows.reshape(
        count_of_rows, KEY_VALUE_HEADS, QUERY_HEADS // KEY_VALUE_HEADS, HEAD_FEATURES
    )
    keys_previous = previous_keys.reshape(
        count_of_rows, context_window, KEY_VALUE_HEADS, HEAD_FEATURES
    )
    values_previous = previous_values.reshape(
        count_of_rows, context_window, KEY_VALUE_HEADS, HEAD_FEATURES
    )
    keys_incoming = incoming_keys.reshape(count_of_rows, -1, KEY_VALUE_HEADS, HEAD_FEATURES)
    values_incoming = incoming_values.reshape(count_of_rows, -1, KEY_VALUE_HEADS, HEAD_FEATURES)
    factor = HEAD_FEATURES ** (-0.5)
    score_old = (
        jnp.einsum(
            "rhgd,rchd->rhgc", grouped_heads, keys_previous, preferred_element_type=jnp.float32
        )
        * factor
    )
    score_new = (
        jnp.einsum(
            "rhgd,rshd->rhgs", grouped_heads, keys_incoming, preferred_element_type=jnp.float32
        )
        * factor
    )
    live_old = (jnp.arange(context_window, dtype=jnp.int32)[None, :] < lengths[:, None])[
        :, None, None, :
    ]
    live_new = (jnp.arange(keys_incoming.shape[1], dtype=jnp.int32) <= step_index)[
        None, None, None, :
    ]
    score_old = jnp.where(live_old, score_old, -1e30)
    score_new = jnp.where(live_new, score_new, -1e30)
    peak_score = jnp.maximum(jnp.max(score_old, axis=-1), jnp.max(score_new, axis=-1))
    weight_old = jnp.where(live_old, jnp.exp(score_old - peak_score[..., None]), 0.0)
    weight_new = jnp.where(live_new, jnp.exp(score_new - peak_score[..., None]), 0.0)
    weight_sum = jnp.sum(weight_old, axis=-1) + jnp.sum(weight_new, axis=-1)
    mixed_out = jnp.einsum(
        "rhgc,rchd->rhgd",
        weight_old.astype(jnp.bfloat16),
        values_previous,
        preferred_element_type=jnp.float32,
    )
    mixed_out = mixed_out + jnp.einsum(
        "rhgs,rshd->rhgd",
        weight_new.astype(jnp.bfloat16),
        values_incoming,
        preferred_element_type=jnp.float32,
    )
    return (mixed_out / weight_sum[..., None]).reshape(count_of_rows, -1).astype(jnp.bfloat16)


def normalize(rows_in, squares, norm_scale):
    factor_rows = lax.rsqrt(squares / D + EPS)
    return (rows_in.astype(jnp.float32) * factor_rows[:, None] * norm_scale[None, :]).astype(
        jnp.bfloat16
    )


def local(
    inputs,
    norm_gain,
    query_weight,
    key_weight,
    value_weight,
    output_weight,
    query_down,
    query_up,
    output_down,
    output_up,
    block_adapter,
    cache_lengths,
    cache_keys,
    cache_values,
):
    across_second = lax.axis_size("gy")
    index_first = lax.axis_index("gx")
    index_second = lax.axis_index("gy")
    request_count = inputs.shape[1] * across_second
    local_rows = cache_keys.shape[0]
    block_count = block_adapter.shape[0]
    norm_scale = norm_gain.astype(jnp.float32)
    query_first = pick_adapters(query_down, block_adapter, index_second * query_down.shape[0])
    query_second = pick_adapters(query_up, block_adapter, index_first * query_up.shape[0])
    output_first = pick_adapters(output_down, block_adapter, index_first * output_down.shape[0])
    output_second = pick_adapters(output_up, block_adapter, index_second * output_up.shape[0])
    incoming_keys = jnp.zeros((local_rows, STEPS, cache_keys.shape[2]), jnp.bfloat16)
    incoming_values = jnp.zeros((local_rows, STEPS, cache_values.shape[2]), jnp.bfloat16)
    results = []
    for step_index in range(STEPS):
        own_inputs = inputs[step_index]
        rows_all = lax.all_gather(own_inputs, "gy", axis=0, tiled=True)
        squares = lax.psum(jnp.sum(jnp.square(rows_all.astype(jnp.float32)), axis=1), "gx")
        normed = normalize(rows_all, squares, norm_scale)
        blocked = normed.reshape(block_count, BLOCK, -1)
        rank_part = jnp.einsum(
            "bnd,bdr->bnr", blocked, query_first, preferred_element_type=jnp.float32
        )
        rank_query = lax.psum(rank_part, ("gx", "gy")).astype(jnp.bfloat16)
        delta_query = jnp.einsum(
            "bnr,bre->bne", rank_query, query_second, preferred_element_type=jnp.float32
        ).reshape(request_count, -1)
        part_query = jnp.dot(normed, query_weight, preferred_element_type=jnp.float32) + delta_query
        part_key = jnp.dot(normed, key_weight, preferred_element_type=jnp.float32)
        part_value = jnp.dot(normed, value_weight, preferred_element_type=jnp.float32)
        summed = (
            lax.psum_scatter(part_query, "gx", scatter_dimension=0, tiled=True),
            lax.psum_scatter(part_key, "gx", scatter_dimension=0, tiled=True),
            lax.psum_scatter(part_value, "gx", scatter_dimension=0, tiled=True),
        )
        query_full, key_complete, value_full = (
            lax.all_to_all(
                summed[0].astype(jnp.bfloat16), "gy", split_axis=0, concat_axis=1, tiled=True
            ),
            lax.all_to_all(
                summed[1].astype(jnp.bfloat16), "gy", split_axis=0, concat_axis=1, tiled=True
            ),
            lax.all_to_all(
                summed[2].astype(jnp.bfloat16), "gy", split_axis=0, concat_axis=1, tiled=True
            ),
        )
        token_positions = cache_lengths + step_index
        query_rot = rotary_embedding(
            query_full.astype(jnp.float32).reshape(local_rows, QUERY_HEADS, HEAD_FEATURES),
            token_positions,
        ).astype(jnp.bfloat16)
        key_rotated = rotary_embedding(
            key_complete.astype(jnp.float32).reshape(local_rows, KEY_VALUE_HEADS, HEAD_FEATURES),
            token_positions,
        ).astype(jnp.bfloat16)
        incoming_keys = incoming_keys.at[:, step_index].set(key_rotated.reshape(local_rows, -1))
        incoming_values = incoming_values.at[:, step_index].set(value_full)
        mixed_local = attend(
            query_rot.reshape(local_rows, -1),
            cache_keys,
            cache_values,
            incoming_keys,
            incoming_values,
            cache_lengths,
            step_index,
        )
        head_group = lax.all_to_all(mixed_local, "gy", split_axis=1, concat_axis=0, tiled=True)
        mixed_all = lax.all_gather(head_group, "gx", axis=0, tiled=True)
        rank_part_out = jnp.einsum(
            "bnq,bqr->bnr",
            mixed_all.reshape(block_count, BLOCK, -1),
            output_first,
            preferred_element_type=jnp.float32,
        )
        rank_output = lax.psum(rank_part_out, ("gx", "gy")).astype(jnp.bfloat16)
        delta_output = jnp.einsum(
            "bnr,bre->bne", rank_output, output_second, preferred_element_type=jnp.float32
        ).reshape(request_count, -1)
        partial_out = (
            jnp.dot(mixed_all, output_weight, preferred_element_type=jnp.float32) + delta_output
        )
        results.append(
            lax.psum_scatter(partial_out, "gy", scatter_dimension=0, tiled=True).astype(
                jnp.bfloat16
            )
        )
    return jnp.stack(results)


def solution(mesh):
    in_specs = (
        P(None, "gy", "gx"),
        P("gx"),
        P("gx", "gy"),
        P("gx", "gy"),
        P("gx", "gy"),
        P("gy", "gx"),
        P("gy", "gx", None),
        P("gx", None, "gy"),
        P("gx", "gy", None),
        P("gy", None, "gx"),
        P(),
        P(("gx", "gy")),
        P(("gx", "gy"), None, None),
        P(("gx", "gy"), None, None),
    )
    out_specs = P(None, "gy", "gx")
    return jax.shard_map(local, mesh=mesh, in_specs=in_specs, out_specs=out_specs, check_vma=False)
```

profile of v0, /device:TPU:0, one launch (start us, length us, event | category | flops | bytes accessed | tf_op | source)
XLA Modules:
  0.0 941.0 jit_solution(17731421883246101163)
XLA Ops:
  7.7 8.6 all-gather.2
  16.3 7.3 all-gather
  23.8 7.3 all-gather.1
  32.3 21.7 %all-reduce.4 = (f32[256]{0:T(256)S(1)}, f32[256]{0:T(256)S(1)}, f32[256]{0:T(256)S(1)}) all-reduce(f32[256]{0:T(256)S(1)} %fusion.66, f32[256]{0:T(256)S(1)} %fusion.69, f32[256]{0:T(256)S(1)} %fusion.72), channel_id=1, replica_groups=mesh['gx'=8,'gy'=4] {'gx'}, use_global_device_ids=true, to_apply=%region_1.0 | all-reduce | flops 768 | bytes 6144 | tf_op jit(solution)/shard_map/psum | solution.py:135
  64.5 11.4 %copy.109 = bf16[4,8,64,2048]{3,1,2,0:T(8,128)(2,1)} copy(bf16[4,8,64,2048]{3,2,1,0:T(8,128)(2,1)} %bitcast.289) | data formatting | bytes 16777216
  75.9 15.6 %copy.74 = bf16[64,1024,64]{2,1,0:T(8,128)(2,1)} copy(bf16[64,1024,64]{1,2,0:T(8,128)(2,1)} %param.32) | data formatting | bytes 16777216 | tf_op args[6]
  91.5 16.5 %reshape.597 = bf16[64,65536]{1,0:T(8,128)(2,1)} reshape(bf16[64,1024,64]{2,1,0:T(8,128)(2,1)} %copy.74) | data formatting | bytes 16777216 | tf_op jit(solution)/shard_map/reshape | solution.py:34
  108.0 4.7 convolution_convert_fusion.3
  114.1 4.7 convolution_convert_fusion.1
  118.7 40.4 %all-reduce.7 = (bf16[2,128,64]{1,2,0:T(8,128)(2,1)S(1)}, bf16[2,128,64]{1,2,0:T(8,128)(2,1)S(1)}, bf16[2,128,64]{1,2,0:T(8,128)(2,1)S(1)}) all-reduce(f32[2,128,64]{1,2,0:T(8,128)S(1)} %fusion.191, f32[2,128,64]{1,2,0:T(8,128)S(1)} %fusion.183, f32[2,128,64]{1,2,0:T(8,128)S(1)} %fusion.187), channel_id=1, replica_groups=mesh['gx'=8,'gy'=4] {'gx','gy'}, use_global_device_ids=true, to_apply=%region_26.27 | all-reduce | flops 49152 | bytes 294912 | tf_op jit(solution)/shard_map/psum | solution.py:141
  159.7 4.8 convolution_add_fusion.1
  165.1 4.9 convolution_add_fusion
  170.5 4.8 convolution_add_fusion.2
  177.0 3.3 all-to-all-start.1
  181.6 60.8 %reduce-scatter.17.cloned.1.call-done = f32[32,256]{1,0:T(8,128)} async-done(((f32[256,256]{1,0:T(8,128)}), f32[32,256]{1,0:T(8,128)}) %reduce-scatter.17.cloned.1.call-update) | async-done | bytes 32784 | tf_op jit(solution)/shard_map/reduce_scatter | solution.py:151
  243.9 62.1 %reduce-scatter.25.cloned.1.call-done = f32[32,256]{1,0:T(8,128)} async-done(((f32[256,256]{1,0:T(8,128)}), f32[32,256]{1,0:T(8,128)}) %reduce-scatter.25.cloned.1.call-update) | async-done | bytes 32784 | tf_op jit(solution)/shard_map/reduce_scatter | solution.py:151
  307.3 62.1 %reduce-scatter.31.cloned.1.call-done = f32[32,256]{1,0:T(8,128)} async-done(((f32[256,256]{1,0:T(8,128)}), f32[32,256]{1,0:T(8,128)}) %reduce-scatter.31.cloned.1.call-update) | async-done | bytes 32784 | tf_op jit(solution)/shard_map/reduce_scatter | solution.py:150
  370.8 62.2 %reduce-scatter.33.cloned.1.call-done = f32[32,256]{1,0:T(8,128)} async-done(((f32[256,256]{1,0:T(8,128)}), f32[32,256]{1,0:T(8,128)}) %reduce-scatter.33.cloned.1.call-update) | async-done | bytes 32784 | tf_op jit(solution)/shard_map/reduce_scatter | solution.py:151
  437.8 3.6 all-to-all-done.5
  444.8 3.7 all-to-all-done.9
  451.8 3.7 all-to-all-done.2
  459.0 3.6 all-to-all-done.6
  462.6 40.5 %reduce-scatter.21.cloned.1.call-done = f32[32,2048]{1,0:T(8,128)} async-done(((f32[256,2048]{1,0:T(8,128)}), f32[32,2048]{1,0:T(8,128)}) %reduce-scatter.21.cloned.1.call-update) | async-done | bytes 262160 | tf_op jit(solution)/shard_map/reduce_scatter | solution.py:149
  504.8 3.3 all-to-all-start.4
  508.1 65.3 %reduce-scatter.29.cloned.1.call-done = f32[32,2048]{1,0:T(8,128)} async-done(((f32[256,2048]{1,0:T(8,128)}), f32[32,2048]{1,0:T(8,128)}) %reduce-scatter.29.cloned.1.call-update) | async-done | bytes 262160 | tf_op jit(solution)/shard_map/reduce_scatter | solution.py:149
  575.0 68.6 %reduce-scatter.13.cloned.1.call-done = f32[32,2048]{1,0:T(8,128)} async-done(((f32[256,2048]{1,0:T(8,128)}), f32[32,2048]{1,0:T(8,128)}) %reduce-scatter.13.cloned.1.call-update) | async-done | bytes 262160 | tf_op jit(solution)/shard_map/reduce_scatter | solution.py:149
  645.3 3.3 all-to-all-start.8
  649.1 4.1 all-to-all-done.8
  657.3 3.7 fusion.181
  663.1 3.3 all-to-all-start
  667.2 3.8 all-to-all-done
  671.5 3.6 fusion.179
  677.0 7.7 all_to_all.174
  688.0 7.7 all_to_all.175
  699.3 7.7 all_to_all.176
  707.1 12.0 %copy.113 = bf16[8,8,64,1024]{3,1,2,0:T(8,128)(2,1)} copy(bf16[8,8,64,1024]{3,2,1,0:T(8,128)(2,1)} %bitcast.290) | data formatting | bytes 16777216
  719.1 15.8 %copy.83 = bf16[32,2048,64]{2,1,0:T(8,128)(2,1)} copy(bf16[32,2048,64]{1,2,0:T(8,128)(2,1)} %param.34) | data formatting | bytes 16777216 | tf_op args[8]
  734.9 15.9 %reshape.608 = bf16[32,131072]{1,0:T(8,128)(2,1)} reshape(bf16[32,2048,64]{2,1,0:T(8,128)(2,1)} %copy.83) | data formatting | bytes 16777216 | tf_op jit(solution)/shard_map/reshape | solution.py:34
  750.8 4.7 convolution_convert_fusion
  756.2 4.7 convolution_convert_fusion.2
  765.9 39.2 %all-gather.7.cloned.1.call-done = bf16[256,2048]{1,0:T(8,128)(2,1)} async-done(((bf16[32,2048]{1,0:T(8,128)(2,1)}), bf16[256,2048]{1,0:T(8,128)(2,1)}) %all-gather.7.cloned.1.call-update) | async-done | bytes 1048592 | tf_op jit(solution)/shard_map/all_gather | solution.py:185
  806.9 41.8 %all-reduce.8 = (bf16[2,128,64]{1,2,0:T(8,128)(2,1)S(1)}, bf16[2,128,64]{1,2,0:T(8,128)(2,1)S(1)}, bf16[2,128,64]{1,2,0:T(8,128)(2,1)S(1)}) all-reduce(f32[2,128,64]{1,2,0:T(8,128)S(1)} %fusion.194, f32[2,128,64]{1,2,0:T(8,128)S(1)} %fusion.190, f32[2,128,64]{1,2,0:T(8,128)S(1)} %fusion.186), channel_id=1, replica_groups=mesh['gx'=8,'gy'=4] {'gx','gy'}, use_global_device_ids=true, to_apply=%region_34.35 | all-reduce | flops 49152 | bytes 294912 | tf_op jit(solution)/shard_map/psum | solution.py:192
  849.1 4.5 convolution_add_fusion.3
  854.0 4.6 convolution_add_fusion.4
  859.0 4.7 convolution_add_fusion.5
  863.8 13.7 %reduce-scatter.35.cloned.1.call-done = f32[64,1024]{1,0:T(8,128)} async-done(((f32[256,1024]{1,0:T(8,128)}), f32[64,1024]{1,0:T(8,128)}) %reduce-scatter.35.cloned.1.call-update) | async-done | bytes 262160 | tf_op jit(solution)/shard_map/reduce_scatter | solution.py:200
  878.4 26.5 %reduce-scatter.27.cloned.1.call-done = f32[64,1024]{1,0:T(8,128)} async-done(((f32[256,1024]{1,0:T(8,128)}), f32[64,1024]{1,0:T(8,128)}) %reduce-scatter.27.cloned.1.call-update) | async-done | bytes 262160 | tf_op jit(solution)/shard_map/reduce_scatter | solution.py:200
  905.9 26.4 %reduce-scatter.19.cloned.1.call-done = f32[64,1024]{1,0:T(8,128)} async-done(((f32[256,1024]{1,0:T(8,128)}), f32[64,1024]{1,0:T(8,128)}) %reduce-scatter.19.cloned.1.call-update) | async-done | bytes 262160 | tf_op jit(solution)/shard_map/reduce_scatter | solution.py:200
  (174 shorter events, 71.6 us)
Async XLA Ops:
  6.5 48.9 %copy-start = (bf16[1024,256]{1,0:T(8,128)(2,1)S(1)}, bf16[1024,256]{1,0:T(8,128)(2,1)}, u32[]{:S(2)}) copy-start(bf16[1024,256]{1,0:T(8,128)(2,1)} %param.29) | copy-start | bytes 1572868
  6.5 25.7 %copy-start.9 = (bf16[1024]{0:T(1024)(128)(2,1)S(1)}, bf16[1024]{0:T(1024)(128)(2,1)}, u32[]{:S(2)}) copy-start(bf16[1024]{0:T(1024)(128)(2,1)} %param.27) | copy-start | bytes 6148
  6.5 169.1 %reduce-scatter.15.cloned.1.call-start = ((), (), s32[]{:S(2)}) async-start(), calls=%async_computation.25 | async-start | bytes 294912 | tf_op jit(solution)/shard_map/reduce_scatter | solution.py:150
  31.1 0.8 copy-start.3
  55.4 7.5 copy-start.4
  56.5 123.8 %reduce-scatter.23.cloned.1.call-start = ((), (), s32[]{:S(2)}) async-start(), calls=%async_computation.30 | async-start | bytes 294912 | tf_op jit(solution)/shard_map/reduce_scatter | solution.py:150
  57.5 185.0 %reduce-scatter.17.cloned.1.call-start = ((), (), s32[]{:S(2)}) async-start(), calls=%async_computation.26 | async-start | bytes 294912 | tf_op jit(solution)/shard_map/reduce_scatter | solution.py:151
  59.7 246.3 %reduce-scatter.25.cloned.1.call-start = ((), (), s32[]{:S(2)}) async-start(), calls=%async_computation.31 | async-start | bytes 294912 | tf_op jit(solution)/shard_map/reduce_scatter | solution.py:151
  61.8 307.7 %reduce-scatter.31.cloned.1.call-start = ((), (), s32[]{:S(2)}) async-start(), calls=%async_computation.35 | async-start | bytes 294912 | tf_op jit(solution)/shard_map/reduce_scatter | solution.py:150
  62.9 370.1 %reduce-scatter.33.cloned.1.call-start = ((), (), s32[]{:S(2)}) async-start(), calls=%async_computation.36 | async-start | bytes 294912 | tf_op jit(solution)/shard_map/reduce_scatter | solution.py:151
  63.9 439.2 %reduce-scatter.21.cloned.1.call-start = ((), (), s32[]{:S(2)}) async-start(), calls=%async_computation.29 | async-start | bytes 2359296 | tf_op jit(solution)/shard_map/reduce_scatter | solution.py:149
  91.5 16.5 %copy-start.8 = (s32[2]{0:T(128)S(1)}, s32[2]{0:T(128)}, u32[]{:S(2)}) copy-start(s32[2]{0:T(128)} %param.36) | copy-start | bytes 28
  164.5 408.9 %reduce-scatter.29.cloned.1.call-start = ((), (), s32[]{:S(2)}) async-start(), calls=%async_computation.34 | async-start | bytes 2359296 | tf_op jit(solution)/shard_map/reduce_scatter | solution.py:149
  169.9 473.7 %reduce-scatter.13.cloned.1.call-start = ((), (), s32[]{:S(2)}) async-start(), calls=%async_computation.24 | async-start | bytes 2359296 | tf_op jit(solution)/shard_map/reduce_scatter | solution.py:149
  170.5 4.9 copy-start.10
  177.0 257.3 %all-to-all-start.1 = ((bf16[4,8,256]{2,1,0:T(8,128)(2,1)}), bf16[4,8,256]{2,1,0:T(8,128)(2,1)S(1)}, u32[]{:S(2)}, u32[]{:S(2)}) async-start(bf16[4,8,256]{2,1,0:T(8,128)(2,1)} %convert_bitcast_fusion.15), calls=%async_computation.3 | async-start | bytes 32768 | tf_op jit(solution)/shard_map/all_to_all | solution.py:157
  434.3 7.1 all-to-all-start.5
  441.4 7.1 all-to-all-start.9
  448.5 7.1 all-to-all-start.2
  455.6 7.1 all-to-all-start.6
  504.8 140.5 %all-to-all-start.4 = ((bf16[4,8,2048]{2,1,0:T(8,128)(2,1)}), bf16[4,8,2048]{2,1,0:T(8,128)(2,1)S(1)}, u32[]{:S(2)}, u32[]{:S(2)}) async-start(bf16[4,8,2048]{2,1,0:T(8,128)(2,1)} %convert_bitcast_fusion.6), calls=%async_computation.9 | async-start | bytes 262144 | tf_op jit(solution)/shard_map/all_to_all | solution.py:154
  645.3 7.9 all-to-all-start.8
  653.2 9.9 %all-to-all-start.10 = ((bf16[4,8,256]{2,1,0:T(8,128)(2,1)}), bf16[4,8,256]{2,1,0:T(8,128)(2,1)S(1)}, u32[]{:S(2)}, u32[]{:S(2)}) async-start(bf16[4,8,256]{2,1,0:T(8,128)(2,1)} %convert_bitcast_fusion.10), calls=%async_computation.21 | async-start | bytes 32768 | tf_op jit(solution)/shard_map/all_to_all | solution.py:160
  656.8 4.3 copy-start.2
  663.1 7.9 all-to-all-start
  666.4 94.4 %all-gather.11.cloned.1.call-start = ((), (), s32[]{:S(2)}) async-start(), calls=%async_computation.37 | async-start | bytes 1179648 | tf_op jit(solution)/shard_map/all_gather | solution.py:185
  671.4 4.8 copy-start.11
  684.7 79.5 %all-gather.9.cloned.1.call-start = ((), (), s32[]{:S(2)}) async-start(), calls=%async_computation.32 | async-start | bytes 1179648 | tf_op jit(solution)/shard_map/all_gather | solution.py:185
  695.7 109.4 %all-gather.7.cloned.1.call-start = ((), (), s32[]{:S(2)}) async-start(), calls=%async_computation.27 | async-start | bytes 1179648 | tf_op jit(solution)/shard_map/all_gather | solution.py:185
  707.0 170.4 %reduce-scatter.35.cloned.1.call-start = ((), (), s32[]{:S(2)}) async-start(), calls=%async_computation.38 | async-start | bytes 1310720 | tf_op jit(solution)/shard_map/reduce_scatter | solution.py:200
  760.9 88.2 %copy-start.5 = (bf16[256,2048]{1,0:T(8,128)(2,1)S(1)}, bf16[256,2048]{1,0:T(8,128)(2,1)}, u32[]{:S(2)}) copy-start(bf16[256,2048]{1,0:T(8,128)(2,1)} %all-gather.11.cloned.1.call-done) | copy-start | bytes 3145732
  849.0 4.9 copy-start.6
  853.6 51.4 %reduce-scatter.27.cloned.1.call-start = ((), (), s32[]{:S(2)}) async-start(), calls=%async_computation.33 | async-start | bytes 1310720 | tf_op jit(solution)/shard_map/reduce_scatter | solution.py:200
  854.0 5.0 copy-start.7
  858.6 73.7 %reduce-scatter.19.cloned.1.call-start = ((), (), s32[]{:S(2)}) async-start(), calls=%async_computation.28 | async-start | bytes 1310720 | tf_op jit(solution)/shard_map/reduce_scatter | solution.py:200
  859.0 75.0 %copy-start.1 = (bf16[1024,256]{1,0:T(8,128)(2,1)S(1)}, bf16[1024,256]{1,0:T(8,128)(2,1)}, u32[]{:S(2)}) copy-start(bf16[1024,256]{1,0:T(8,128)(2,1)} %param.29) | copy-start | bytes 1572868
Sparse Core Ops, SparseCore 0:
  56.6 58.5 reduce-scatter.14
  118.5 60.3 reduce-scatter.22
  182.2 60.2 reduce-scatter.16
  245.7 60.2 reduce-scatter.24
  309.2 60.2 reduce-scatter.30
  372.6 60.2 reduce-scatter.32
  436.5 66.6 reduce-scatter.20
  506.7 66.6 reduce-scatter.28
  576.9 66.6 reduce-scatter.12
  684.8 38.2 all-gather.10
  725.3 38.8 all-gather.8
  766.2 38.8 all-gather.6
  853.7 23.7 reduce-scatter.34
  880.0 24.8 reduce-scatter.26
  907.3 24.9 reduce-scatter.18
where the time goes:
time: 947 us; the launch traced here: 941 us
  waiting for transfers between devices  552 us (58%)
  blocking collectives  150 us (16%)
  local copies, waits for them, and re-layouts  91.7 us (10%)
  matrix products  81.2 us (9%)
  starting transfers between devices  30.7 us (3%)
  other arithmetic  21.1 us (2%)
  between operations  14.5 us (2%)
    reduce_scatter x3, waiting for transfers between devices, local(): lax.psum_scatter(part_value, 'gx', scatter_dimension=0, tiled=True)  185 us
    reduce_scatter x3, waiting for transfers between devices, local(): lax.psum_scatter(part_query, 'gx', scatter_dimension=0, tiled=True)  174 us
    reduce_scatter x3, waiting for transfers between devices, local(): lax.psum_scatter(partial_out, 'gy', scatter_dimension=0, tiled=True)  66.6 us
    reduce_scatter x3, waiting for transfers between devices, local(): lax.psum_scatter(part_key, 'gx', scatter_dimension=0, tiled=True)  62.2 us
    unnamed x34, local copies, waits for them, and re-layouts  55.8 us
    psum x1, blocking collectives, local(): rank_output = lax.psum(rank_part_out, ('gx', 'gy')).astype(jnp.bfloat16)  41.8 us
    all_gather x3, waiting for transfers between devices, local(): mixed_all = lax.all_gather(head_group, 'gx', axis=0, tiled=True)  40.7 us
    psum x1, blocking collectives, local(): rank_query = lax.psum(rank_part, ('gx', 'gy')).astype(jnp.bfloat16)  40.4 us
  transfers between devices with their start and end apart: 24, of which 18 were waited for; matrix products, arithmetic and copies ran while one was open for 19% of the time, Pallas kernels for 0%

commit v1 on v0

--- a/solution.py
+++ b/solution.py
@@ -1,3 +1,4 @@
+import functools
 import jax
 import jax.numpy as jnp
 from jax import lax
@@ -11,6 +12,13 @@
 STEPS = 3
 EPS = 1e-05
 THETA = 500000.0
+
+
+def fit_tables(values, dev_axis, row_axis):
+    return lax.psum(lax.psum(values, dev_axis), row_axis)
+
+
+target_supply_all = functools.partial(fit_tables, dev_axis="gy", row_axis="gx")
 
 
 def rotary_embedding(values_in, token_positions):
@@ -138,7 +146,7 @@
         rank_part = jnp.einsum(
             "bnd,bdr->bnr", blocked, query_first, preferred_element_type=jnp.float32
         )
-        rank_query = lax.psum(rank_part, ("gx", "gy")).astype(jnp.bfloat16)
+        rank_query = target_supply_all(rank_part).astype(jnp.bfloat16)
         delta_query = jnp.einsum(
             "bnr,bre->bne", rank_query, query_second, preferred_element_type=jnp.float32
         ).reshape(request_count, -1)

time: 947 us -> 1000 us (1.056)
  waiting for transfers between devices: 552 us -> 600 us
    reduce_scatter x3, waiting for transfers between devices: 62.2 us -> 99.8 us  [local(): lax.psum_scatter(part_key, 'gx', scatter_dimension=0, tiled=True)]
    unnamed x34 -> x36, local copies, waits for them, and re-layouts: 55.8 us -> 56.4 us
  transfers between devices with their start and end apart: 24 -> 25, of which waited for: 18 -> 20; matrix products, arithmetic and copies ran while one was open for 19% -> 14% of each run, Pallas kernels for 0% -> 0%
where the time goes in v1:
time: 1000 us; the launch traced here: 991 us
  waiting for transfers between devices  600 us (60%)
  blocking collectives  149 us (15%)
  local copies, waits for them, and re-layouts  92.4 us (9%)
  matrix products  81 us (8%)
  starting transfers between devices  30.7 us (3%)
  other arithmetic  21.2 us (2%)
  between operations  15.7 us (2%)
    reduce_scatter x3, waiting for transfers between devices, local(): lax.psum_scatter(part_value, 'gx', scatter_dimension=0, tiled=True)  188 us
    reduce_scatter x3, waiting for transfers between devices, local(): lax.psum_scatter(part_query, 'gx', scatter_dimension=0, tiled=True)  176 us
    reduce_scatter x3, waiting for transfers between devices, local(): lax.psum_scatter(part_key, 'gx', scatter_dimension=0, tiled=True)  99.8 us
    reduce_scatter x3, waiting for transfers between devices, local(): lax.psum_scatter(partial_out, 'gy', scatter_dimension=0, tiled=True)  66.8 us
    unnamed x36, local copies, waits for them, and re-layouts  56.4 us
    psum x1, blocking collectives, local(): rank_output = lax.psum(rank_part_out, ('gx', 'gy')).astype(jnp.bfloat16)  41.5 us
    all_gather x3, waiting for transfers between devices, local(): mixed_all = lax.all_gather(head_group, 'gx', axis=0, tiled=True)  41.3 us
    psum x1, blocking collectives, fit_tables(): return lax.psum(lax.psum(values, dev_axis), row_axis)  39.8 us
  transfers between devices with their start and end apart: 25, of which 20 were waited for; matrix products, arithmetic and copies ran while one was open for 14% of the time, Pallas kernels for 0%

profile of v1, /device:TPU:0, one launch (start us, length us, event | category | flops | bytes accessed | tf_op | source)
XLA Modules:
  0.0 990.7 jit_solution(10025358102399825124)
XLA Ops:
  8.5 8.6 all-gather.2
  17.2 7.3 all-gather
  25.4 7.3 all-gather.1
  33.9 21.7 %all-reduce.4 = (f32[256]{0:T(256)S(1)}, f32[256]{0:T(256)S(1)}, f32[256]{0:T(256)S(1)}) all-reduce(f32[256]{0:T(256)S(1)} %fusion.66, f32[256]{0:T(256)S(1)} %fusion.69, f32[256]{0:T(256)S(1)} %fusion.72), channel_id=1, replica_groups=mesh['gx'=8,'gy'=4] {'gx'}, use_global_device_ids=true, to_apply=%region_1.0 | all-reduce | flops 768 | bytes 6144 | tf_op jit(solution)/shard_map/psum | solution.py:143
  55.6 15.5 %copy.74 = bf16[64,1024,64]{2,1,0:T(8,128)(2,1)} copy(bf16[64,1024,64]{1,2,0:T(8,128)(2,1)} %param.32) | data formatting | bytes 16777216 | tf_op args[6]
  71.1 16.5 %reshape.597 = bf16[64,65536]{1,0:T(8,128)(2,1)} reshape(bf16[64,1024,64]{2,1,0:T(8,128)(2,1)} %copy.74) | data formatting | bytes 16777216 | tf_op jit(solution)/shard_map/reshape | solution.py:42
  87.7 4.6 convolution_convert_fusion.3
  104.3 11.4 %copy.109 = bf16[4,8,64,2048]{3,1,2,0:T(8,128)(2,1)} copy(bf16[4,8,64,2048]{3,2,1,0:T(8,128)(2,1)} %bitcast.289) | data formatting | bytes 16777216
  115.7 4.7 convolution_convert_fusion.1
  120.5 5.9 all-reduce.10.cloned.1.call-done
  126.3 39.8 %all-reduce.11 = (bf16[2,128,64]{1,2,0:T(8,128)(2,1)S(1)}, bf16[2,128,64]{1,2,0:T(8,128)(2,1)S(1)}, bf16[2,128,64]{1,2,0:T(8,128)(2,1)S(1)}) all-reduce(f32[2,128,64]{1,2,0:T(8,128)} %get-tuple-element.89, f32[2,128,64]{1,2,0:T(8,128)} %get-tuple-element.90, f32[2,128,64]{1,2,0:T(8,128)} %get-tuple-element.91), channel_id=1, replica_groups=mesh['gx'=8,'gy'=4] {'gx'}, use_global_device_ids=true, to_apply=%region_29.30 | all-reduce | flops 49152 | bytes 294912 | tf_op jit(solution)/shard_map/psum | solution.py:18
  166.7 4.8 convolution_add_fusion.1
  172.1 4.8 convolution_add_fusion
  177.6 4.8 convolution_add_fusion.2
  187.3 37.0 %reduce-scatter.23.cloned.1.call-done = f32[32,256]{1,0:T(8,128)} async-done(((f32[256,256]{1,0:T(8,128)}), f32[32,256]{1,0:T(8,128)}) %reduce-scatter.23.cloned.1.call-update) | async-done | bytes 32784 | tf_op jit(solution)/shard_map/reduce_scatter | solution.py:158
  225.6 62.6 %reduce-scatter.17.cloned.1.call-done = f32[32,256]{1,0:T(8,128)} async-done(((f32[256,256]{1,0:T(8,128)}), f32[32,256]{1,0:T(8,128)}) %reduce-scatter.17.cloned.1.call-update) | async-done | bytes 32784 | tf_op jit(solution)/shard_map/reduce_scatter | solution.py:159
  289.6 62.7 %reduce-scatter.25.cloned.1.call-done = f32[32,256]{1,0:T(8,128)} async-done(((f32[256,256]{1,0:T(8,128)}), f32[32,256]{1,0:T(8,128)}) %reduce-scatter.25.cloned.1.call-update) | async-done | bytes 32784 | tf_op jit(solution)/shard_map/reduce_scatter | solution.py:159
  353.7 62.8 %reduce-scatter.31.cloned.1.call-done = f32[32,256]{1,0:T(8,128)} async-done(((f32[256,256]{1,0:T(8,128)}), f32[32,256]{1,0:T(8,128)}) %reduce-scatter.31.cloned.1.call-update) | async-done | bytes 32784 | tf_op jit(solution)/shard_map/reduce_scatter | solution.py:158
  417.8 62.8 %reduce-scatter.33.cloned.1.call-done = f32[32,256]{1,0:T(8,128)} async-done(((f32[256,256]{1,0:T(8,128)}), f32[32,256]{1,0:T(8,128)}) %reduce-scatter.33.cloned.1.call-update) | async-done | bytes 32784 | tf_op jit(solution)/shard_map/reduce_scatter | solution.py:159
  485.5 3.6 all-to-all-done.5
  492.4 3.7 all-to-all-done.9
  496.1 3.4 all-to-all-start.2
  499.7 3.7 all-to-all-done.2
  506.8 3.6 all-to-all-done.6
  510.4 40.9 %reduce-scatter.21.cloned.1.call-done = f32[32,2048]{1,0:T(8,128)} async-done(((f32[256,2048]{1,0:T(8,128)}), f32[32,2048]{1,0:T(8,128)}) %reduce-scatter.21.cloned.1.call-update) | async-done | bytes 262160 | tf_op jit(solution)/shard_map/reduce_scatter | solution.py:157
  556.3 65.7 %reduce-scatter.29.cloned.1.call-done = f32[32,2048]{1,0:T(8,128)} async-done(((f32[256,2048]{1,0:T(8,128)}), f32[32,2048]{1,0:T(8,128)}) %reduce-scatter.29.cloned.1.call-update) | async-done | bytes 262160 | tf_op jit(solution)/shard_map/reduce_scatter | solution.py:157
  623.7 68.9 %reduce-scatter.13.cloned.1.call-done = f32[32,2048]{1,0:T(8,128)} async-done(((f32[256,2048]{1,0:T(8,128)}), f32[32,2048]{1,0:T(8,128)}) %reduce-scatter.13.cloned.1.call-update) | async-done | bytes 262160 | tf_op jit(solution)/shard_map/reduce_scatter | solution.py:157
  698.0 4.1 all-to-all-done.8
  706.2 3.7 fusion.181
  711.9 3.3 all-to-all-start
  715.9 4.0 all-to-all-done
  720.4 3.6 fusion.179
  725.9 7.7 all_to_all.174
  736.9 7.7 all_to_all.175
  748.2 7.7 all_to_all.176
  755.9 11.9 %copy.113 = bf16[8,8,64,1024]{3,1,2,0:T(8,128)(2,1)} copy(bf16[8,8,64,1024]{3,2,1,0:T(8,128)(2,1)} %bitcast.290) | data formatting | bytes 16777216
  767.9 15.8 %copy.83 = bf16[32,2048,64]{2,1,0:T(8,128)(2,1)} copy(bf16[32,2048,64]{1,2,0:T(8,128)(2,1)} %param.34) | data formatting | bytes 16777216 | tf_op args[8]
  783.6 15.9 %reshape.608 = bf16[32,131072]{1,0:T(8,128)(2,1)} reshape(bf16[32,2048,64]{2,1,0:T(8,128)(2,1)} %copy.83) | data formatting | bytes 16777216 | tf_op jit(solution)/shard_map/reshape | solution.py:42
  799.6 4.7 convolution_convert_fusion
  804.9 4.7 convolution_convert_fusion.2
  814.9 39.6 %all-gather.7.cloned.1.call-done = bf16[256,2048]{1,0:T(8,128)(2,1)} async-done(((bf16[32,2048]{1,0:T(8,128)(2,1)}), bf16[256,2048]{1,0:T(8,128)(2,1)}) %all-gather.7.cloned.1.call-update) | async-done | bytes 1048592 | tf_op jit(solution)/shard_map/all_gather | solution.py:193
  856.2 41.5 %all-reduce.12 = (bf16[2,128,64]{1,2,0:T(8,128)(2,1)S(1)}, bf16[2,128,64]{1,2,0:T(8,128)(2,1)S(1)}, bf16[2,128,64]{1,2,0:T(8,128)(2,1)S(1)}) all-reduce(f32[2,128,64]{1,2,0:T(8,128)S(1)} %fusion.194, f32[2,128,64]{1,2,0:T(8,128)S(1)} %fusion.190, f32[2,128,64]{1,2,0:T(8,128)S(1)} %fusion.186), channel_id=1, replica_groups=mesh['gx'=8,'gy'=4] {'gx','gy'}, use_global_device_ids=true, to_apply=%region_37.38 | all-reduce | flops 49152 | bytes 294912 | tf_op jit(solution)/shard_map/psum | solution.py:200
  898.1 4.5 convolution_add_fusion.3
  903.1 4.5 convolution_add_fusion.4
  908.1 4.7 convolution_add_fusion.5
  912.8 13.8 %reduce-scatter.35.cloned.1.call-done = f32[64,1024]{1,0:T(8,128)} async-done(((f32[256,1024]{1,0:T(8,128)}), f32[64,1024]{1,0:T(8,128)}) %reduce-scatter.35.cloned.1.call-update) | async-done | bytes 262160 | tf_op jit(solution)/shard_map/reduce_scatter | solution.py:208
  927.6 26.5 %reduce-scatter.27.cloned.1.call-done = f32[64,1024]{1,0:T(8,128)} async-done(((f32[256,1024]{1,0:T(8,128)}), f32[64,1024]{1,0:T(8,128)}) %reduce-scatter.27.cloned.1.call-update) | async-done | bytes 262160 | tf_op jit(solution)/shard_map/reduce_scatter | solution.py:208
  955.0 26.5 %reduce-scatter.19.cloned.1.call-done = f32[64,1024]{1,0:T(8,128)} async-done(((f32[256,1024]{1,0:T(8,128)}), f32[64,1024]{1,0:T(8,128)}) %reduce-scatter.19.cloned.1.call-update) | async-done | bytes 262160 | tf_op jit(solution)/shard_map/reduce_scatter | solution.py:208
  (179 shorter events, 79.1 us)
Async XLA Ops:
  7.4 89.9 %copy-start = (bf16[1024,256]{1,0:T(8,128)(2,1)S(1)}, bf16[1024,256]{1,0:T(8,128)(2,1)}, u32[]{:S(2)}) copy-start(bf16[1024,256]{1,0:T(8,128)(2,1)} %param.29) | copy-start | bytes 1572868
  7.4 26.6 %copy-start.10 = (bf16[1024]{0:T(1024)(128)(2,1)S(1)}, bf16[1024]{0:T(1024)(128)(2,1)}, u32[]{:S(2)}) copy-start(bf16[1024]{0:T(1024)(128)(2,1)} %param.27) | copy-start | bytes 6148
  7.4 119.0 %all-reduce.10.cloned.1.call-start = ((), (), s32[]{:S(2)}) async-start(), calls=%async_computation.39 | async-start | bytes 393216 | tf_op jit(solution)/shard_map/psum | solution.py:18
  24.4 0.8 copy-start.3
  32.7 0.8 copy-start.4
  71.1 16.6 %copy-start.9 = (s32[2]{0:T(128)S(1)}, s32[2]{0:T(128)}, u32[]{:S(2)}) copy-start(s32[2]{0:T(128)} %param.36) | copy-start | bytes 28
  94.3 5.1 copy-start.5
  97.2 85.4 %reduce-scatter.15.cloned.1.call-start = ((), (), s32[]{:S(2)}) async-start(), calls=%async_computation.25 | async-start | bytes 294912 | tf_op jit(solution)/shard_map/reduce_scatter | solution.py:158
  98.3 125.9 %reduce-scatter.23.cloned.1.call-start = ((), (), s32[]{:S(2)}) async-start(), calls=%async_computation.30 | async-start | bytes 294912 | tf_op jit(solution)/shard_map/reduce_scatter | solution.py:158
  99.4 188.9 %reduce-scatter.17.cloned.1.call-start = ((), (), s32[]{:S(2)}) async-start(), calls=%async_computation.26 | async-start | bytes 294912 | tf_op jit(solution)/shard_map/reduce_scatter | solution.py:159
  100.5 251.9 %reduce-scatter.25.cloned.1.call-start = ((), (), s32[]{:S(2)}) async-start(), calls=%async_computation.31 | async-start | bytes 294912 | tf_op jit(solution)/shard_map/reduce_scatter | solution.py:159
  101.6 314.9 %reduce-scatter.31.cloned.1.call-start = ((), (), s32[]{:S(2)}) async-start(), calls=%async_computation.35 | async-start | bytes 294912 | tf_op jit(solution)/shard_map/reduce_scatter | solution.py:158
  102.7 377.9 %reduce-scatter.33.cloned.1.call-start = ((), (), s32[]{:S(2)}) async-start(), calls=%async_computation.36 | async-start | bytes 294912 | tf_op jit(solution)/shard_map/reduce_scatter | solution.py:159
  103.8 447.6 %reduce-scatter.21.cloned.1.call-start = ((), (), s32[]{:S(2)}) async-start(), calls=%async_computation.29 | async-start | bytes 2359296 | tf_op jit(solution)/shard_map/reduce_scatter | solution.py:157
  171.5 450.5 %reduce-scatter.29.cloned.1.call-start = ((), (), s32[]{:S(2)}) async-start(), calls=%async_computation.34 | async-start | bytes 2359296 | tf_op jit(solution)/shard_map/reduce_scatter | solution.py:157
  172.0 4.9 copy-start.11
  176.9 515.6 %reduce-scatter.13.cloned.1.call-start = ((), (), s32[]{:S(2)}) async-start(), calls=%async_computation.24 | async-start | bytes 2359296 | tf_op jit(solution)/shard_map/reduce_scatter | solution.py:157
  184.0 298.0 %all-to-all-start.1 = ((bf16[4,8,256]{2,1,0:T(8,128)(2,1)}), bf16[4,8,256]{2,1,0:T(8,128)(2,1)S(1)}, u32[]{:S(2)}, u32[]{:S(2)}) async-start(bf16[4,8,256]{2,1,0:T(8,128)(2,1)} %convert_bitcast_fusion.15), calls=%async_computation.3 | async-start | bytes 32768 | tf_op jit(solution)/shard_map/all_to_all | solution.py:165
  482.0 7.1 all-to-all-start.5
  489.0 7.1 all-to-all-start.9
  496.1 7.3 all-to-all-start.2
  503.4 7.1 all-to-all-start.6
  553.0 141.1 %all-to-all-start.4 = ((bf16[4,8,2048]{2,1,0:T(8,128)(2,1)}), bf16[4,8,2048]{2,1,0:T(8,128)(2,1)S(1)}, u32[]{:S(2)}, u32[]{:S(2)}) async-start(bf16[4,8,2048]{2,1,0:T(8,128)(2,1)} %convert_bitcast_fusion.6), calls=%async_computation.9 | async-start | bytes 262144 | tf_op jit(solution)/shard_map/all_to_all | solution.py:162
  694.1 7.9 all-to-all-start.8
  702.1 9.9 all-to-all-start.10
  705.7 4.3 copy-start.2
  711.9 7.9 all-to-all-start
  715.3 94.3 %all-gather.11.cloned.1.call-start = ((), (), s32[]{:S(2)}) async-start(), calls=%async_computation.37 | async-start | bytes 1179648 | tf_op jit(solution)/shard_map/all_gather | solution.py:193
  720.2 4.8 copy-start.12
  733.6 79.6 %all-gather.9.cloned.1.call-start = ((), (), s32[]{:S(2)}) async-start(), calls=%async_computation.32 | async-start | bytes 1179648 | tf_op jit(solution)/shard_map/all_gather | solution.py:193
  744.5 109.9 %all-gather.7.cloned.1.call-start = ((), (), s32[]{:S(2)}) async-start(), calls=%async_computation.27 | async-start | bytes 1179648 | tf_op jit(solution)/shard_map/all_gather | solution.py:193
  755.9 170.7 %reduce-scatter.35.cloned.1.call-start = ((), (), s32[]{:S(2)}) async-start(), calls=%async_computation.38 | async-start | bytes 1310720 | tf_op jit(solution)/shard_map/reduce_scatter | solution.py:208
  809.6 88.5 %copy-start.6 = (bf16[256,2048]{1,0:T(8,128)(2,1)S(1)}, bf16[256,2048]{1,0:T(8,128)(2,1)}, u32[]{:S(2)}) copy-start(bf16[256,2048]{1,0:T(8,128)(2,1)} %all-gather.11.cloned.1.call-done) | copy-start | bytes 3145732
  898.1 4.9 copy-start.7
  902.7 51.4 %reduce-scatter.27.cloned.1.call-start = ((), (), s32[]{:S(2)}) async-start(), calls=%async_computation.33 | async-start | bytes 1310720 | tf_op jit(solution)/shard_map/reduce_scatter | solution.py:208
  903.1 5.0 copy-start.8
  907.7 73.9 %reduce-scatter.19.cloned.1.call-start = ((), (), s32[]{:S(2)}) async-start(), calls=%async_computation.28 | async-start | bytes 1310720 | tf_op jit(solution)/shard_map/reduce_scatter | solution.py:208
  908.1 75.3 %copy-start.1 = (bf16[1024,256]{1,0:T(8,128)(2,1)S(1)}, bf16[1024,256]{1,0:T(8,128)(2,1)}, u32[]{:S(2)}) copy-start(bf16[1024,256]{1,0:T(8,128)(2,1)} %param.29) | copy-start | bytes 1572868
Sparse Core Ops, SparseCore 0:
  97.3 28.9 all-reduce.9
  902.8 23.7 reduce-scatter.34
  929.1 24.9 reduce-scatter.26
  956.6 24.8 reduce-scatter.18
Sparse Core Ops, SparseCore 1:
  101.4 58.7 reduce-scatter.14
  163.7 60.5 reduce-scatter.22
  227.8 60.4 reduce-scatter.16
  292.0 60.3 reduce-scatter.24
  356.1 60.4 reduce-scatter.30
  420.2 60.4 reduce-scatter.32
  484.4 66.9 reduce-scatter.20
  555.2 66.8 reduce-scatter.28
  625.8 66.6 reduce-scatter.12
  733.7 38.3 all-gather.10
  774.2 38.9 all-gather.8
  815.5 38.9 all-gather.6
